TPU v7x, 128 devices: a whole 4x4x4 slice. The times are simulated.
128 devices in a mesh: dp: 16 (over y, x_lo, core), feat: 8 (over x_hi, z).
Axes of the slice: x: 4 (x_hi: 2, x_lo: 2; x = x_hi * 2 + x_lo), y: 4, z: 4, core: 2. Of those that a mesh axis runs over, the one named last changes fastest.
Arguments:
- dataset: bfloat16 [131072, 4096], P('dp', 'feat'), may hold values from -0.09375 to 0.09375
- targets: float32 [131072], P('dp'), may hold values from 0 to 1
- indices: int32 [32768], P('dp'), may hold values from 0 to 8191
- particles: bfloat16 [1536, 4096], P('dp', 'feat'), may hold values from -6 to 6
- spread: int32 [1], replicated, may hold values from 2048 to 8191
Outputs:
- attraction: float32 [1536, 4096], P('dp', 'feat')
- repulsion: float32 [1536, 4096], P('dp', 'feat')
Inputs may be any that keep to these rules, and one draw needn't show every extreme that they name: Entry r of indices names a row within block r // 2048 of the dataset's blocks of 8192 rows.
All inputs are finite; a program needn't handle non-finite values.
Results may differ from a plain program's by a relative error of at most 0.00115.
Values may be sent and summed in bfloat16 or wider, within the bound.
No kernel may reach another device: no remote copies, remote signals or barrier semaphores. Data moves between devices by JAX's collectives and lax.ppermute only.
A program may use at most 128 MiB of HBM per device.

v0:
```python
import jax
import jax.numpy as jnp
from jax import lax
from jax.sharding import PartitionSpec as P


def contract(left, right):
    return lax.dot_general(
        left, right, (((1,), (1,)), ((), ())), preferred_element_type=jnp.float32
    )


def exact_dot(left, right):
    return jnp.dot(left, right, precision=lax.Precision.HIGHEST)


def body(dataset, targets, indices, particles, spread):
    batch_x = jnp.take(dataset, indices, axis=0)
    batch_t = jnp.take(targets, indices, axis=0)
    data_ratio = dataset.shape[0] / indices.shape[0]
    scale_h = spread[0].astype(jnp.float32)
    all_rows = lax.all_gather(particles, "dp", axis=0, tiled=True)
    count_all = all_rows.shape[0]
    partial_value = contract(batch_x, all_rows)
    own_logits = lax.psum_scatter(
        partial_value.astype(jnp.bfloat16), "feat", scatter_dimension=1, tiled=True
    ).astype(jnp.float32)
    own_residual = (batch_t[:, None] - jax.nn.sigmoid(own_logits)).astype(jnp.bfloat16)
    residual = lax.all_gather(own_residual, "feat", axis=1, tiled=True)
    gradient = lax.psum_scatter(
        lax.dot_general(
            residual, batch_x, (((0,), (0,)), ((), ())), preferred_element_type=jnp.float32
        ),
        "dp",
        scatter_dimension=0,
        tiled=True,
    )
    theta_own = particles.astype(jnp.float32)
    score = data_ratio * gradient - theta_own
    group_score, group_theta = (
        lax.all_gather(score, "feat", axis=1, tiled=True),
        lax.all_gather(theta_own, "feat", axis=1, tiled=True),
    )
    rows_own = particles.shape[0] // lax.axis_size("feat")
    own_start = lax.axis_index("feat") * rows_own
    theta_f = lax.dynamic_slice_in_dim(group_theta, own_start, rows_own, 0)
    own_sq = jnp.sum(theta_f * theta_f, axis=1)
    theta_b = lax.all_gather(group_theta, "dp", axis=0, tiled=True)
    score_b = lax.all_gather(group_score, "dp", axis=0, tiled=True)
    norms_b = jnp.sum(theta_b * theta_b, axis=1)
    inner = lax.dot_general(
        theta_f, theta_b, (((1,), (1,)), ((), ())), precision=lax.Precision.HIGHEST
    )
    kernel = jnp.exp(-(own_sq[:, None] + norms_b[None, :] - 2.0 * inner) / scale_h)
    pushed = exact_dot(kernel, score_b)
    pulled = exact_dot(kernel, theta_b)
    weight = jnp.sum(kernel, axis=1)
    attraction = pushed / count_all
    repulsion = (theta_f * weight[:, None] - pulled) / count_all
    return (
        lax.all_to_all(attraction, "feat", split_axis=1, concat_axis=0, tiled=True),
        lax.all_to_all(repulsion, "feat", split_axis=1, concat_axis=0, tiled=True),
    )


def solution(mesh):
    return jax.shard_map(
        body,
        mesh=mesh,
        in_specs=(P("dp", "feat"), P("dp"), P("dp"), P("dp", "feat"), P()),
        out_specs=(P("dp", "feat"), P("dp", "feat")),
        check_vma=False,
    )
```

profile of v0, /device:TPU:0, one launch (start us, length us, event | category | flops | bytes accessed | tf_op | source)
XLA Modules:
  0.0 722.8 jit_solution(17134586862805063873)
XLA Ops:
  7.2 0.0 copy-start
  7.2 0.0 all-gather.11.cloned.1.call-start
  7.2 0.7 all-gather.11.cloned.1.call-update
  7.9 0.0 reduce-scatter.7.cloned.1.call-start
  8.0 0.7 fusion.8
  8.7 11.8 %gather_fusion = f32[2048]{0:T(1024)S(1)} fusion(f32[8192]{0:T(1024)S(1)} %copy-done, s32[2048]{0:T(1024)S(1)} %fusion.8), kind=kCustom, calls=%fused_computation | custom fusion | bytes 24576 | tf_op jit(solution)/shard_map/jit(_take)/gather | solution.py:19
  20.5 12.1 %gather_fusion.1 = bf16[2048,512]{1,0:T(8,128)(2,1)S(1)} fusion(bf16[8192,512]{1,0:T(8,128)(2,1)} %param.5, s32[2048]{0:T(1024)S(1)} %fusion.8), kind=kCustom, calls=%fused_computation.1 | custom fusion | bytes 4202496 | tf_op jit(solution)/shard_map/jit(_take)/gather | solution.py:18
  32.6 12.7 %all-gather.11.cloned.1.call-done = bf16[1536,512]{1,0:T(8,128)(2,1)} async-done(((bf16[96,512]{1,0:T(8,128)(2,1)}), bf16[1536,512]{1,0:T(8,128)(2,1)}) %all-gather.11.cloned.1.call-update) | async-done | bytes 1572880 | tf_op jit(solution)/shard_map/all_gather | solution.py:22
  45.3 7.0 fusion
  52.3 0.0 reduce-scatter.7.cloned.1.call-update
  52.3 0.0 all-gather.13.cloned.1.call-start
  52.4 98.1 %reduce-scatter.7.cloned.1.call-done = bf16[192,2048]{1,0:T(8,128)(2,1)} async-done(((bf16[1536,2048]{1,0:T(8,128)(2,1)}), bf16[192,2048]{1,0:T(8,128)(2,1)}) %reduce-scatter.7.cloned.1.call-update) | async-done | bytes 786448
  150.5 2.4 subtract_convert_fusion
  152.9 0.0 all-gather.13.cloned.1.call-update
  153.0 0.0 reduce-scatter.5.cloned.1.call-start
  153.0 87.3 %all-gather.13.cloned.1.call-done = bf16[2048,1536]{0,1:T(8,128)(2,1)} async-done(((bf16[2048,192]{0,1:T(8,128)(2,1)}), bf16[2048,1536]{0,1:T(8,128)(2,1)}) %all-gather.13.cloned.1.call-update) | async-done | bytes 6291472 | tf_op jit(solution)/shard_map/all_gather | solution.py:29
  240.3 8.0 %fusion.6 = f32[1536,512]{1,0:T(8,128)} fusion(bf16[2048,1536]{0,1:T(8,128)(2,1)} %all-gather.13.cloned.1.call-done, bf16[2048,512]{1,0:T(8,128)(2,1)S(1)} %gather_fusion.1, pred[2048]{0:T(1024)(128)(4,1)S(1)} %get-tuple-element.3), kind=kOutput, calls=%fused_computation.15 | convolution fusion | flops 3222274048 | bytes 11536384 | tf_op jit(solution)/shard_map/dot_general | solution.py:31
  248.4 0.0 reduce-scatter.5.cloned.1.call-update
  248.4 0.0 all-gather.7.cloned.1.call-start
  248.4 0.8 copy-done.3
  249.3 0.7 convert_element_type.18
  249.9 0.0 all-gather.7.cloned.1.call-update
  250.0 0.0 all-gather.15.cloned.1.call-start
  250.0 63.5 %reduce-scatter.5.cloned.1.call-done = f32[96,512]{1,0:T(8,128)} async-done(((f32[1536,512]{1,0:T(8,128)}), f32[96,512]{1,0:T(8,128)}) %reduce-scatter.5.cloned.1.call-update) | async-done | bytes 196624 | tf_op jit(solution)/shard_map/reduce_scatter | solution.py:30
  313.5 1.6 multiply_subtract_fusion
  315.1 0.0 all-gather.15.cloned.1.call-update
  315.2 0.0 all-gather.9.cloned.1.call-start
  315.2 49.5 %all-gather.7.cloned.1.call-done = f32[96,4096]{1,0:T(8,128)} async-done(((f32[96,512]{1,0:T(8,128)}), f32[96,4096]{1,0:T(8,128)}) %all-gather.7.cloned.1.call-update) | async-done | bytes 1572880 | tf_op jit(solution)/shard_map/all_gather | solution.py:42
  364.7 0.0 all-gather.9.cloned.1.call-update
  364.7 0.2 all-gather.17.cloned.1.call-start
  364.9 50.7 %all-gather.15.cloned.1.call-done = f32[96,4096]{1,0:T(8,128)} async-done(((f32[96,512]{1,0:T(8,128)}), f32[96,4096]{1,0:T(8,128)}) %all-gather.15.cloned.1.call-update) | async-done | bytes 1572880 | tf_op jit(solution)/shard_map/all_gather | solution.py:41
  415.6 0.0 all-gather.17.cloned.1.call-update
  416.3 0.2 multiply_reduce_fusion.1
  416.5 130.7 %all-gather.9.cloned.1.call-done = f32[1536,4096]{1,0:T(8,128)} async-done(((f32[96,4096]{1,0:T(8,128)}), f32[1536,4096]{1,0:T(8,128)}) %all-gather.9.cloned.1.call-update) | async-done | bytes 25165840 | tf_op jit(solution)/shard_map/all_gather | solution.py:48
  547.2 9.4 %multiply_reduce_fusion = f32[1536]{0:T(1024)S(1)} fusion(f32[1536,4096]{1,0:T(8,128)} %all-gather.9.cloned.1.call-done), kind=kLoop, calls=%fused_computation.2 | loop fusion | flops 12581376 | bytes 25171968 | tf_op jit(solution)/shard_map/reduce_sum | solution.py:50
  556.6 24.9 %fusion.12 = (f32[12]{0:T(128)S(1)}, f32[12,1536]{1,0:T(8,128)S(1)}) fusion(f32[]{:T(128)} %bitcast, f32[1536,4096]{1,0:T(8,128)} %all-gather.9.cloned.1.call-done, f32[96,4096]{1,0:T(8,128)S(1)} %copy-done.2, s32[]{:T(128)S(6)} %select_n.20, f32[1536]{0:T(1024)S(1)} %multiply_reduce_fusion, f32[12]{0:T(128)S(1)} %multiply_reduce_fusion.1), kind=kOutput, calls=%fused_computation.26 | convolution fusion | flops 906080256 | bytes 25510456 | tf_op jit(solution)/shard_map/dot_general | solution.py:51
  581.5 15.3 %fusion.1 = f32[12,4096]{1,0:T(8,128)S(1)} fusion(f32[12,1536]{1,0:T(8,128)S(1)} %get-tuple-element.5, f32[1536,4096]{1,0:T(8,128)} %all-gather.9.cloned.1.call-done, f32[96,4096]{1,0:T(8,128)S(1)} %copy-done.2, s32[]{:T(128)S(6)} %select_n.20, f32[12]{0:T(128)S(1)} %get-tuple-element.4), kind=kOutput, calls=%fused_computation.7 | convolution fusion | flops 906117120 | bytes 25632820 | tf_op jit(solution)/shard_map/dot_general | solution.py:14
  596.8 0.2 copy.22
  597.0 0.8 copy.18
  597.8 6.7 all-to-all-start.1
  604.5 78.9 %all-gather.17.cloned.1.call-done = f32[1536,4096]{1,0:T(8,128)} async-done(((f32[96,4096]{1,0:T(8,128)}), f32[1536,4096]{1,0:T(8,128)}) %all-gather.17.cloned.1.call-update) | async-done | bytes 25165840 | tf_op jit(solution)/shard_map/all_gather | solution.py:49
  683.4 15.1 %convolution_multiply_fusion = f32[12,4096]{1,0:T(8,128)S(1)} fusion(f32[12,1536]{1,0:T(8,128)S(1)} %get-tuple-element.5, f32[1536,4096]{1,0:T(8,128)} %all-gather.17.cloned.1.call-done), kind=kOutput, calls=%fused_computation.6 | convolution fusion | flops 906018816 | bytes 25436160 | tf_op jit(solution)/shard_map/dot_general | solution.py:14
  698.5 0.2 copy.21
  698.7 0.8 copy.17
  699.5 6.5 all-to-all-start
  706.1 0.7 all_to_all.35
  706.8 8.4 %all-to-all-done = f32[12,8,512]{2,0,1:T(8,128)S(1)} async-done(((f32[12,8,512]{2,0,1:T(8,128)}), f32[12,8,512]{2,0,1:T(8,128)S(1)}, u32[]{:S(2)}, u32[]{:S(2)}) %all-to-all-start) | async-done | bytes 196640 | tf_op jit(solution)/shard_map/all_to_all | solution.py:61
  715.2 0.7 all_to_all.31
  (12 shorter events, 0.1 us)
Async XLA Ops:
  7.2 1.5 copy-start
  7.2 38.1 %all-gather.11.cloned.1.call-start = ((), (), s32[]{:S(2)}) async-start(), calls=%async_computation.6 | async-start | bytes 1671168 | tf_op jit(solution)/shard_map/all_gather | solution.py:22
  7.9 142.6 %reduce-scatter.7.cloned.1.call-start = ((), (), s32[]{:S(2)}) async-start(), calls=%async_computation.11 | async-start | bytes 7077888
  20.5 12.1 %copy-start.4 = (s32[2048]{0:T(1024)S(1)}, s32[2048]{0:T(1024)}, u32[]{:S(2)}) copy-start(s32[2048]{0:T(1024)} %param.7) | copy-start | bytes 24580
  52.3 188.0 %all-gather.13.cloned.1.call-start = ((), (), s32[]{:S(2)}) async-start(), calls=%async_computation.7 | async-start | bytes 7077888 | tf_op jit(solution)/shard_map/all_gather | solution.py:29
  153.0 160.5 %reduce-scatter.5.cloned.1.call-start = ((), (), s32[]{:S(2)}) async-start(), calls=%async_computation.8 | async-start | bytes 3342336 | tf_op jit(solution)/shard_map/reduce_scatter | solution.py:30
  248.4 0.9 copy-start.3
  248.4 116.3 %all-gather.7.cloned.1.call-start = ((), (), s32[]{:S(2)}) async-start(), calls=%async_computation.4 | async-start | bytes 1769472 | tf_op jit(solution)/shard_map/all_gather | solution.py:42
  250.0 165.7 %all-gather.15.cloned.1.call-start = ((), (), s32[]{:S(2)}) async-start(), calls=%async_computation.9 | async-start | bytes 1769472 | tf_op jit(solution)/shard_map/all_gather | solution.py:41
  315.2 232.0 %all-gather.9.cloned.1.call-start = ((), (), s32[]{:S(2)}) async-start(), calls=%async_computation.5 | async-start | bytes 26738688 | tf_op jit(solution)/shard_map/all_gather | solution.py:48
  364.7 51.6 %copy-start.2 = (f32[96,4096]{1,0:T(8,128)S(1)}, f32[96,4096]{1,0:T(8,128)}, u32[]{:S(2)}) copy-start(f32[96,4096]{1,0:T(8,128)} %all-gather.7.cloned.1.call-done) | copy-start | bytes 4718596
  364.7 318.7 %all-gather.17.cloned.1.call-start = ((), (), s32[]{:S(2)}) async-start(), calls=%async_computation.10 | async-start | bytes 26738688 | tf_op jit(solution)/shard_map/all_gather | solution.py:49
  597.8 101.7 %all-to-all-start.1 = ((f32[12,8,512]{2,0,1:T(8,128)}), f32[12,8,512]{2,0,1:T(8,128)S(1)}, u32[]{:S(2)}, u32[]{:S(2)}) async-start(f32[12,8,512]{2,0,1:T(8,128)} %copy.18), calls=%async_computation.2 | async-start | bytes 524288 | tf_op jit(solution)/shard_map/all_to_all | solution.py:62
  683.4 32.5 %copy-start.1 = (f32[8192]{0:T(1024)S(1)}, f32[8192]{0:T(1024)}, u32[]{:S(2)}) copy-start(f32[8192]{0:T(1024)} %param.6) | copy-start | bytes 98308
  699.5 15.7 %all-to-all-start = ((f32[12,8,512]{2,0,1:T(8,128)}), f32[12,8,512]{2,0,1:T(8,128)S(1)}, u32[]{:S(2)}, u32[]{:S(2)}) async-start(f32[12,8,512]{2,0,1:T(8,128)} %copy.17), calls=%async_computation.1 | async-start | bytes 524288 | tf_op jit(solution)/shard_map/all_to_all | solution.py:61
Sparse Core Ops, SparseCore 0:
  9.7 35.5 all-gather.10
  52.4 97.9 reduce-scatter.6
  153.1 87.2 all-gather.12
  248.5 64.9 reduce-scatter.4
  316.2 48.4 all-gather.6
  367.4 48.1 all-gather.14
  417.3 129.7 all-gather.8
  548.9 134.5 all-gather.16
where the time goes:
time: 723 us
  waiting for transfers between devices  581 us (80%)
  matrix products  70.3 us (10%)
  local copies, waits for them, and re-layouts  28.1 us (4%)
  other arithmetic  15.1 us (2%)
  between operations  14.9 us (2%)
  starting transfers between devices  13.8 us (2%)
    all_gather x1, waiting for transfers between devices, body(): theta_b = lax.all_gather(group_theta, 'dp', axis=0, tiled=True)  131 us
    unnamed x9, waiting for transfers between devices  98.9 us
    all_gather x1, waiting for transfers between devices, body(): residual = lax.all_gather(own_residual, 'feat', axis=1, tiled=True)  87.3 us
    all_gather x1, waiting for transfers between devices, body(): score_b = lax.all_gather(group_score, 'dp', axis=0, tiled=True)  78.9 us
    reduce_scatter x1, waiting for transfers between devices, body(): lax.psum_scatter(lax.dot_general(residual, batch_x, (((0,), (0,)), ((), (...  63.5 us
    all_gather x1, waiting for transfers between devices, body(): lax.all_gather(score, 'feat', axis=1, tiled=True)  50.7 us
    all_gather x1, waiting for transfers between devices, body(): lax.all_gather(theta_own, 'feat', axis=1, tiled=True)  49.5 us
    dot_general x2, matrix products, exact_dot(): return jnp.dot(left, right, precision=lax.Precision.HIGHEST)  30.3 us
  transfers between devices with their start and end apart: 10, of which 9 were waited for; matrix products, arithmetic and copies ran while one was open for 13% of the time, Pallas kernels for 0%

commit v1 on v0

v1 whole, which is shorter than its diff:
```python
import jax
import jax.numpy as jnp
from jax import lax
from jax.sharding import PartitionSpec as P


def contract(left, right):
    return lax.dot_general(
        left, right, (((1,), (1,)), ((), ())), preferred_element_type=jnp.float32
    )


def exact_dot(left, right):
    return jnp.dot(left, right, precision=lax.Precision.HIGHEST)


def body(dataset, targets, indices, particles, spread):
    batch_x = jnp.take(dataset, indices, axis=0)
    batch_t = jnp.take(targets, indices, axis=0)
    data_ratio = dataset.shape[0] / indices.shape[0]
    scale_h = spread[0].astype(jnp.float32)
    all_rows = lax.all_gather(particles, "dp", axis=0, tiled=True)
    count_all = all_rows.shape[0]
    rows_own = particles.shape[0]
    inner_part = contract(particles, all_rows)
    theta_all = all_rows.astype(jnp.float32)
    sq_part = jnp.sum(theta_all * theta_all, axis=1)
    packed = lax.psum(jnp.concatenate([inner_part, sq_part[None, :]], axis=0), "feat")
    inner = packed[:rows_own]
    norms_b = packed[rows_own]
    own_sq = lax.dynamic_slice_in_dim(norms_b, lax.axis_index("dp") * rows_own, rows_own, 0)
    partial_value = contract(batch_x, all_rows)
    own_logits = lax.psum_scatter(
        partial_value.astype(jnp.bfloat16), "feat", scatter_dimension=1, tiled=True
    ).astype(jnp.float32)
    own_residual = (batch_t[:, None] - jax.nn.sigmoid(own_logits)).astype(jnp.bfloat16)
    residual = lax.all_gather(own_residual, "feat", axis=1, tiled=True)
    gradient = lax.psum(
        lax.dot_general(
            residual, batch_x, (((0,), (0,)), ((), ())), preferred_element_type=jnp.float32
        ),
        "dp",
    )
    score = data_ratio * gradient - theta_all
    kernel = jnp.exp(-(own_sq[:, None] + norms_b[None, :] - 2.0 * inner) / scale_h)
    pushed = exact_dot(kernel, score)
    pulled = exact_dot(kernel, theta_all)
    weight = jnp.sum(kernel, axis=1)
    attraction = pushed / count_all
    repulsion = (particles.astype(jnp.float32) * weight[:, None] - pulled) / count_all
    return attraction, repulsion


def solution(mesh):
    return jax.shard_map(
        body,
        mesh=mesh,
        in_specs=(P("dp", "feat"), P("dp"), P("dp"), P("dp", "feat"), P()),
        out_specs=(P("dp", "feat"), P("dp", "feat")),
        check_vma=False,
    )
```

time: 723 us -> 471 us (0.65)
  waiting for transfers between devices: 581 us -> 398 us
  matrix products: 70.3 us -> 25.2 us
  starting transfers between devices: 13.8 us -> 0.38 us
  other arithmetic: 15.1 us -> 5.89 us
    all_gather x4 -> x0, waiting for transfers between devices: 310 us -> none  [the longest x1 131 us: body(): theta_b = lax.all_gather(group_theta, 'dp', axis=0, tiled=True)]
    psum x0 -> x2, waiting for transfers between devices: none -> 203 us  [the longest x1 126 us: body(): lax.psum(lax.dot_general(residual, batch_x, (((0,), (0,)), ((), ())), pre...]
    reduce_scatter x1 -> x0, waiting for transfers between devices: 63.5 us -> none  [body(): lax.psum_scatter(lax.dot_general(residual, batch_x, (((0,), (0,)), ((), (...]
    dot_general x1 -> x0, matrix products: 24.9 us -> none  [body(): lax.dot_general(theta_f, theta_b, (((1,), (1,)), ((), ())), precision=lax...]
    dot_general x2, matrix products: 30.3 us -> 7.71 us  [exact_dot(): return jnp.dot(left, right, precision=lax.Precision.HIGHEST)]
    all_to_all x2 -> x0, starting transfers between devices: 13.3 us -> none  [the longest x1 6.73 us: body(): lax.all_to_all(repulsion, 'feat', split_axis=1, concat_axis=0, tiled=True)]
    all_to_all x2 -> x0, waiting for transfers between devices: 8.44 us -> none  [the longest x1 8.43 us: body(): lax.all_to_all(attraction, 'feat', split_axis=1, concat_axis=0, tiled=True)]
    reduce_sum x2, other arithmetic: 9.58 us -> 1.76 us  [the longest x1 1.39 us: body(): weight = jnp.sum(kernel, axis=1)]
  transfers between devices with their start and end apart: 10 -> 5, of which waited for: 9 -> 5; matrix products, arithmetic and copies ran while one was open for 13% -> 9% of each run, Pallas kernels for 0% -> 0%
where the time goes in v1:
time: 471 us
  waiting for transfers between devices  398 us (85%)
  local copies, waits for them, and re-layouts  26.4 us (6%)
  matrix products  25.2 us (5%)
  between operations  14.5 us (3%)
  other arithmetic  5.89 us (1%)
    psum x1, waiting for transfers between devices, body(): lax.psum(lax.dot_general(residual, batch_x, (((0,), (0,)), ((), ())), pre...  126 us
    unnamed x6, waiting for transfers between devices  98.8 us
    all_gather x1, waiting for transfers between devices, body(): residual = lax.all_gather(own_residual, 'feat', axis=1, tiled=True)  85.1 us
    psum x1, waiting for transfers between devices, body(): lax.psum(jnp.concatenate([inner_part, sq_part[None, :]], axis=0), 'feat')  77.3 us
    gather x1, local copies, waits for them, and re-layouts, body(): batch_x = jnp.take(dataset, indices, axis=0)  13.7 us
    gather x1, local copies, waits for them, and re-layouts, body(): batch_t = jnp.take(targets, indices, axis=0)  11.8 us
    all_gather x1, waiting for transfers between devices, body(): all_rows = lax.all_gather(particles, 'dp', axis=0, tiled=True)  11.1 us
  transfers between devices with their start and end apart: 5, of which 5 were waited for; matrix products, arithmetic and copies ran while one was open for 9% of the time, Pallas kernels for 0%

profile of v1, /device:TPU:0, one launch (start us, length us, event | category | flops | bytes accessed | tf_op | source)
XLA Modules:
  0.0 470.8 jit_solution(16620537094908766250)
XLA Ops:
  7.2 0.0 copy-start
  7.2 0.0 all-gather.3.cloned.1.call-start
  7.2 0.7 all-gather.3.cloned.1.call-update
  7.9 0.0 reduce-scatter.4.cloned.1.call-start
  8.0 0.7 fusion.12
  8.7 13.7 %gather_fusion.1 = bf16[2048,512]{1,0:T(8,128)(2,1)} fusion(bf16[8192,512]{1,0:T(8,128)(2,1)} %param.5, s32[2048]{0:T(1024)S(1)} %fusion.12), kind=kCustom, calls=%fused_computation.1 | custom fusion | bytes 4202496 | tf_op jit(solution)/shard_map/jit(_take)/gather | solution.py:18
  22.4 0.0 copy-done
  22.4 0.0 copy-start.4
  22.4 11.8 %gather_fusion = f32[2048]{0:T(1024)S(1)} fusion(f32[8192]{0:T(1024)S(1)} %copy-done, s32[2048]{0:T(1024)S(1)} %fusion.12), kind=kCustom, calls=%fused_computation | custom fusion | bytes 24576 | tf_op jit(solution)/shard_map/jit(_take)/gather | solution.py:19
  34.2 0.0 copy-done.4
  34.2 11.1 %all-gather.3.cloned.1.call-done = bf16[1536,512]{1,0:T(8,128)(2,1)} async-done(((bf16[96,512]{1,0:T(8,128)(2,1)}), bf16[1536,512]{1,0:T(8,128)(2,1)}) %all-gather.3.cloned.1.call-update) | async-done | bytes 1572880 | tf_op jit(solution)/shard_map/all_gather | solution.py:22
  45.3 8.2 %fusion = bf16[1536,2048]{1,0:T(8,128)(2,1)} fusion(bf16[1536,512]{1,0:T(8,128)(2,1)} %all-gather.3.cloned.1.call-done, bf16[2048,512]{1,0:T(8,128)(2,1)} %gather_fusion.1, pred[2048]{0:T(1024)(128)(4,1)S(1)} %get-tuple-element.3), kind=kOutput, calls=%fused_computation.3 | convolution fusion | flops 3225419776 | bytes 9963520 | tf_op jit(solution)/shard_map/dot_general | solution.py:8
  53.6 0.0 reduce-scatter.4.cloned.1.call-update
  53.6 0.0 copy-start.1
  53.6 0.0 copy-start.3
  53.6 0.0 all-gather.5.cloned.1.call-start
  53.7 98.0 %reduce-scatter.4.cloned.1.call-done = bf16[192,2048]{1,0:T(8,128)(2,1)} async-done(((bf16[1536,2048]{1,0:T(8,128)(2,1)}), bf16[192,2048]{1,0:T(8,128)(2,1)}) %reduce-scatter.4.cloned.1.call-update) | async-done | bytes 786448
  151.7 2.5 subtract_convert_fusion
  154.2 0.0 all-gather.5.cloned.1.call-update
  154.2 0.0 all-reduce.3.cloned.1.call-start
  154.3 0.0 copy-done.1
  154.3 0.4 fusion.1
  154.7 0.0 copy-done.3
  154.7 0.6 fusion.20
  155.3 0.9 pad_maximum_fusion
  156.2 0.0 all-reduce.3.cloned.1.call-update
  156.2 0.2 all-reduce.5.cloned.1.call-start
  156.5 85.1 %all-gather.5.cloned.1.call-done = bf16[2048,1536]{0,1:T(8,128)(2,1)} async-done(((bf16[2048,192]{0,1:T(8,128)(2,1)}), bf16[2048,1536]{0,1:T(8,128)(2,1)}) %all-gather.5.cloned.1.call-update) | async-done | bytes 6291472 | tf_op jit(solution)/shard_map/all_gather | solution.py:37
  241.6 8.6 %fusion.7 = f32[1536,512]{1,0:T(8,128)} fusion(bf16[2048,1536]{0,1:T(8,128)(2,1)} %all-gather.5.cloned.1.call-done, bf16[2048,512]{1,0:T(8,128)(2,1)} %gather_fusion.1, pred[2048]{0:T(1024)(128)(4,1)S(1)} %get-tuple-element.3), kind=kOutput, calls=%fused_computation.15 | convolution fusion | flops 3222274048 | bytes 11536384 | tf_op jit(solution)/shard_map/dot_general | solution.py:39
  250.2 0.0 all-reduce.5.cloned.1.call-update
  250.9 77.3 %all-reduce.3.cloned.1.call-done = f32[97,1536]{1,0:T(8,128)} async-done(((f32[97,1536]{1,0:T(8,128)}), f32[97,1536]{1,0:T(8,128)}) %all-reduce.3.cloned.1.call-update) | async-done | bytes 595984 | tf_op jit(solution)/shard_map/psum | solution.py:28
  328.2 0.8 fusion.19
  329.0 0.1 dynamic-slice_bitcast_fusion
  329.1 1.4 fusion.17
  330.5 0.0 copy-start.2
  330.5 2.8 fusion.6
  333.3 126.1 %all-reduce.5.cloned.1.call-done = f32[1536,512]{1,0:T(8,128)} async-done(((f32[1536,512]{1,0:T(8,128)}), f32[1536,512]{1,0:T(8,128)}) %all-reduce.5.cloned.1.call-update) | async-done | bytes 3145744 | tf_op jit(solution)/shard_map/psum | solution.py:38
  459.4 0.0 copy-done.2
  459.4 4.9 %fusion.5 = f32[96,512]{1,0:T(8,128)} fusion(bf16[1536,512]{1,0:T(8,128)(2,1)S(1)} %copy-done.1, f32[1536,512]{1,0:T(8,128)} %all-reduce.5.cloned.1.call-done, f32[97,1536]{1,0:T(8,128)S(1)} %copy-done.2, f32[]{:T(128)} %bitcast.1, f32[1536]{0:T(1024)S(1)} %get-tuple-element.5, f32[96]{0:T(128)S(1)} %dynamic-slice_bitcast_fusion), kind=kOutput, calls=%fused_computation.12 | convolution fusion | flops 909115392 | bytes 5513732 | tf_op jit(solution)/shard_map/dot_general | solution.py:14
  (2 shorter events, 0.0 us)
Async XLA Ops:
  7.2 15.2 %copy-start = (f32[8192]{0:T(1024)S(1)}, f32[8192]{0:T(1024)}, u32[]{:S(2)}) copy-start(f32[8192]{0:T(1024)} %param.6) | copy-start | bytes 98308
  7.2 38.1 %all-gather.3.cloned.1.call-start = ((), (), s32[]{:S(2)}) async-start(), calls=%async_computation.1 | async-start | bytes 1671168 | tf_op jit(solution)/shard_map/all_gather | solution.py:22
  7.9 143.8 %reduce-scatter.4.cloned.1.call-start = ((), (), s32[]{:S(2)}) async-start(), calls=%async_computation.5 | async-start | bytes 7077888
  22.4 11.8 %copy-start.4 = (s32[2048]{0:T(1024)S(1)}, s32[2048]{0:T(1024)}, u32[]{:S(2)}) copy-start(s32[2048]{0:T(1024)} %param.7) | copy-start | bytes 24580
  53.6 100.7 %copy-start.1 = (bf16[1536,512]{1,0:T(8,128)(2,1)S(1)}, bf16[1536,512]{1,0:T(8,128)(2,1)}, u32[]{:S(2)}) copy-start(bf16[1536,512]{1,0:T(8,128)(2,1)} %all-gather.3.cloned.1.call-done) | copy-start | bytes 4718596
  53.6 101.1 %copy-start.3 = (bf16[96,512]{1,0:T(8,128)(2,1)S(1)}, bf16[96,512]{1,0:T(8,128)(2,1)}, u32[]{:S(2)}) copy-start(bf16[96,512]{1,0:T(8,128)(2,1)} %param.8) | copy-start | bytes 294916
  53.6 188.0 %all-gather.5.cloned.1.call-start = ((), (), s32[]{:S(2)}) async-start(), calls=%async_computation.3 | async-start | bytes 7077888 | tf_op jit(solution)/shard_map/all_gather | solution.py:37
  154.2 174.0 %all-reduce.3.cloned.1.call-start = ((), (), s32[]{:S(2)}) async-start(), calls=%async_computation.2 | async-start | bytes 1277952 | tf_op jit(solution)/shard_map/psum | solution.py:28
  156.2 303.2 %all-reduce.5.cloned.1.call-start = ((), (), s32[]{:S(2)}) async-start(), calls=%async_computation.4 | async-start | bytes 6291456 | tf_op jit(solution)/shard_map/psum | solution.py:38
  330.5 128.9 %copy-start.2 = (f32[97,1536]{1,0:T(8,128)S(1)}, f32[97,1536]{1,0:T(8,128)}, u32[]{:S(2)}) copy-start(f32[97,1536]{1,0:T(8,128)} %all-reduce.3.cloned.1.call-done) | copy-start | bytes 1787908
Sparse Core Ops, SparseCore 0:
  9.7 35.5 all-gather.2
  53.7 97.9 reduce-scatter.3
  154.4 87.1 all-gather.4
  243.9 84.1 all-reduce.2
  330.6 128.7 all-reduce.4

commit v2 on v1

--- a/solution.py
+++ b/solution.py
@@ -15,6 +15,7 @@
 
 
 def body(dataset, targets, indices, particles, spread):
+    n_feat = lax.axis_size("feat")
     batch_x = jnp.take(dataset, indices, axis=0)
     batch_t = jnp.take(targets, indices, axis=0)
     data_ratio = dataset.shape[0] / indices.shape[0]
@@ -29,17 +30,17 @@
     inner = packed[:rows_own]
     norms_b = packed[rows_own]
     own_sq = lax.dynamic_slice_in_dim(norms_b, lax.axis_index("dp") * rows_own, rows_own, 0)
-    partial_value = contract(batch_x, all_rows)
-    own_logits = lax.psum_scatter(
-        partial_value.astype(jnp.bfloat16), "feat", scatter_dimension=1, tiled=True
-    ).astype(jnp.float32)
-    own_residual = (batch_t[:, None] - jax.nn.sigmoid(own_logits)).astype(jnp.bfloat16)
-    residual = lax.all_gather(own_residual, "feat", axis=1, tiled=True)
-    gradient = lax.psum(
-        lax.dot_general(
-            residual, batch_x, (((0,), (0,)), ((), ())), preferred_element_type=jnp.float32
-        ),
-        "dp",
+    partial_t = contract(all_rows, batch_x).astype(jnp.bfloat16)
+    partial_t = partial_t.reshape(n_feat, count_all // n_feat, partial_t.shape[1])
+    pieces = lax.all_to_all(partial_t, "feat", 0, 0, tiled=True)
+    own_logits_t = jnp.sum(pieces.astype(jnp.float32), axis=0)
+    own_residual_t = (batch_t[None, :] - jax.nn.sigmoid(own_logits_t)).astype(jnp.bfloat16)
+    spread_res = jnp.broadcast_to(own_residual_t[None], (n_feat,) + own_residual_t.shape)
+    residual_t = lax.all_to_all(spread_res, "feat", 0, 0, tiled=True).reshape(count_all, -1)
+    grad_part = jnp.dot(residual_t, batch_x, preferred_element_type=jnp.float32)
+    gradient = lax.all_gather(
+        lax.psum_scatter(grad_part, "dp", scatter_dimension=0, tiled=True),
+        "dp", axis=0, tiled=True,
     )
     score = data_ratio * gradient - theta_all
     kernel = jnp.exp(-(own_sq[:, None] + norms_b[None, :] - 2.0 * inner) / scale_h)

time: 471 us -> 414 us (0.88)
  waiting for transfers between devices: 398 us -> 191 us
  blocking collectives: 0 us -> 156 us
  matrix products: 25.2 us -> 18.7 us
    all_to_all x0 -> x2, blocking collectives: none -> 156 us  [the longest x1 79.9 us: body(): pieces = lax.all_to_all(partial_t, 'feat', 0, 0, tiled=True)]
    psum x1 -> x0, waiting for transfers between devices: 126 us -> none  [body(): lax.psum(lax.dot_general(residual, batch_x, (((0,), (0,)), ((), ())), pre...]
    unnamed x6 -> x4, waiting for transfers between devices: 98.8 us -> 0.73 us
    reduce_scatter x0 -> x1, waiting for transfers between devices: none -> 61.1 us  [body(): lax.psum_scatter(grad_part, 'dp', scatter_dimension=0, tiled=True)]
    all_gather x1, waiting for transfers between devices: 85.1 us -> 29.7 us  [body(): lax.all_gather(lax.psum_scatter(grad_part, 'dp', scatter_dimension=0, til...]
    psum x1, waiting for transfers between devices: 77.3 us -> 86.8 us  [body(): lax.psum(jnp.concatenate([inner_part, sq_part[None, :]], axis=0), 'feat')]
  transfers between devices with their start and end apart: 5 -> 4, of which waited for: 5 -> 4; matrix products, arithmetic and copies ran while one was open for 9% -> 8% of each run, Pallas kernels for 0% -> 0%
where the time goes in v2:
time: 414 us; the launch traced here: 412 us
  waiting for transfers between devices  191 us (46%)
  blocking collectives  156 us (38%)
  local copies, waits for them, and re-layouts  26.9 us (6%)
  matrix products  18.7 us (5%)
  between operations  14.5 us (4%)
  other arithmetic  4.98 us (1%)
    psum x1, waiting for transfers between devices, body(): lax.psum(jnp.concatenate([inner_part, sq_part[None, :]], axis=0), 'feat')  86.8 us
    all_to_all x1, blocking collectives, body(): pieces = lax.all_to_all(partial_t, 'feat', 0, 0, tiled=True)  79.9 us
    all_to_all x1, blocking collectives, body(): lax.all_to_all(spread_res, 'feat', 0, 0, tiled=True).reshape(count_all, -1)  75.9 us
    reduce_scatter x1, waiting for transfers between devices, body(): lax.psum_scatter(grad_part, 'dp', scatter_dimension=0, tiled=True)  61.1 us
    all_gather x1, waiting for transfers between devices, body(): lax.all_gather(lax.psum_scatter(grad_part, 'dp', scatter_dimension=0, til...  29.7 us
    all_gather x1, waiting for transfers between devices, body(): all_rows = lax.all_gather(particles, 'dp', axis=0, tiled=True)  12.8 us
    gather x1, local copies, waits for them, and re-layouts, body(): batch_x = jnp.take(dataset, indices, axis=0)  12 us
    gather x1, local copies, waits for them, and re-layouts, body(): batch_t = jnp.take(targets, indices, axis=0)  11.8 us
  transfers between devices with their start and end apart: 4, of which 4 were waited for; matrix products, arithmetic and copies ran while one was open for 8% of the time, Pallas kernels for 0%

profile of v2, /device:TPU:0, one launch (start us, length us, event | category | flops | bytes accessed | tf_op | source)
XLA Modules:
  0.0 412.5 jit_solution(13167088793554479781)
XLA Ops:
  7.2 0.0 copy-start
  7.2 0.0 all-gather.3.cloned.1.call-start
  7.2 0.7 all-gather.3.cloned.1.call-update
  7.9 0.0 reduce-scatter.2.cloned.1.call-start
  8.0 0.7 fusion.11
  8.7 12.0 %gather_fusion.1 = bf16[2048,512]{1,0:T(8,128)(2,1)S(1)} fusion(bf16[8192,512]{1,0:T(8,128)(2,1)} %param.5, s32[2048]{0:T(1024)S(1)} %fusion.11), kind=kCustom, calls=%fused_computation.1 | custom fusion | bytes 4202496 | tf_op jit(solution)/shard_map/jit(_take)/gather | solution.py:19
  20.7 0.0 copy-done
  20.7 0.0 copy-start.4
  20.7 11.8 %gather_fusion = f32[2048]{0:T(1024)S(1)} fusion(f32[8192]{0:T(1024)S(1)} %copy-done, s32[2048]{0:T(1024)S(1)} %fusion.11), kind=kCustom, calls=%fused_computation | custom fusion | bytes 24576 | tf_op jit(solution)/shard_map/jit(_take)/gather | solution.py:20
  32.5 0.0 copy-done.4
  32.6 12.8 %all-gather.3.cloned.1.call-done = bf16[1536,512]{1,0:T(8,128)(2,1)} async-done(((bf16[96,512]{1,0:T(8,128)(2,1)}), bf16[1536,512]{1,0:T(8,128)(2,1)}) %all-gather.3.cloned.1.call-update) | async-done | bytes 1572880 | tf_op jit(solution)/shard_map/all_gather | solution.py:23
  45.3 5.3 %convolution_convert_fusion = bf16[2048,1536]{0,1:T(8,128)(2,1)S(1)} fusion(bf16[1536,512]{1,0:T(8,128)(2,1)} %all-gather.3.cloned.1.call-done, bf16[2048,512]{1,0:T(8,128)(2,1)S(1)} %gather_fusion.1, pred[2048]{0:T(1024)(128)(4,1)S(1)} %get-tuple-element.3), kind=kOutput, calls=%fused_computation.3 | convolution fusion | flops 3225419776 | bytes 9963520 | tf_op jit(solution)/shard_map/dot_general | solution.py:8
  50.6 79.9 %all_to_all.10 = bf16[8,192,2048]{2,1,0:T(8,128)(2,1)S(1)} all-to-all(bf16[8,192,2048]{2,1,0:T(8,128)(2,1)S(1)} %bitcast.13), channel_id=1, replica_groups=mesh['dp'=16,'feat'=8] {'feat'}, dimensions={0} | all-to-all | bytes 12582912 | tf_op jit(solution)/shard_map/all_to_all | solution.py:35
  130.5 1.2 convert_reduce_fusion
  131.7 0.4 subtract_convert_fusion
  132.1 0.8 broadcast_in_dim.35
  132.9 75.9 %all_to_all.11 = bf16[8,192,2048]{2,1,0:T(8,128)(2,1)S(1)} all-to-all(bf16[8,192,2048]{2,1,0:T(8,128)(2,1)S(1)} %broadcast_in_dim.35), channel_id=1, replica_groups=mesh['dp'=16,'feat'=8] {'feat'}, dimensions={0} | all-to-all | bytes 12582912 | tf_op jit(solution)/shard_map/all_to_all | solution.py:39
  208.8 5.2 %fusion.6 = f32[1536,512]{1,0:T(8,128)} fusion(bf16[1536,2048]{1,0:T(8,128)(2,1)S(1)} %bitcast.12, bf16[2048,512]{1,0:T(8,128)(2,1)S(1)} %gather_fusion.1, pred[2048]{0:T(1024)(128)(4,1)S(1)} %get-tuple-element.3), kind=kOutput, calls=%fused_computation.15 | convolution fusion | flops 3222274048 | bytes 11536384 | tf_op jit(solution)/shard_map/dot_general | solution.py:40
  214.0 0.0 copy-start.1
  214.0 0.0 copy-start.3
  214.0 0.0 reduce-scatter.2.cloned.1.call-update
  214.0 0.0 all-reduce.2.cloned.1.call-start
  214.1 1.3 copy-done.1
  215.4 0.4 fusion
  215.8 0.0 copy-done.3
  215.8 0.6 fusion.19
  216.4 0.9 pad_maximum_fusion
  217.3 0.0 all-reduce.2.cloned.1.call-update
  217.3 0.2 all-gather.5.cloned.1.call-start
  217.5 61.1 %reduce-scatter.2.cloned.1.call-done = f32[96,512]{1,0:T(8,128)} async-done(((f32[1536,512]{1,0:T(8,128)}), f32[96,512]{1,0:T(8,128)}) %reduce-scatter.2.cloned.1.call-update) | async-done | bytes 196624 | tf_op jit(solution)/shard_map/reduce_scatter | solution.py:42
  278.7 0.0 all-gather.5.cloned.1.call-update
  279.4 86.8 %all-reduce.2.cloned.1.call-done = f32[97,1536]{1,0:T(8,128)} async-done(((f32[97,1536]{1,0:T(8,128)}), f32[97,1536]{1,0:T(8,128)}) %all-reduce.2.cloned.1.call-update) | async-done | bytes 595984 | tf_op jit(solution)/shard_map/psum | solution.py:29
  366.2 0.8 fusion.18
  367.0 0.1 dynamic-slice_bitcast_fusion
  367.1 1.4 fusion.16
  368.5 0.0 copy-start.2
  368.5 2.8 fusion.5
  371.3 29.7 %all-gather.5.cloned.1.call-done = f32[1536,512]{1,0:T(8,128)} async-done(((f32[96,512]{1,0:T(8,128)}), f32[1536,512]{1,0:T(8,128)}) %all-gather.5.cloned.1.call-update) | async-done | bytes 3145744 | tf_op jit(solution)/shard_map/all_gather | solution.py:41
  401.0 0.0 copy-done.2
  401.0 4.9 %fusion.4 = f32[96,512]{1,0:T(8,128)} fusion(bf16[1536,512]{1,0:T(8,128)(2,1)S(1)} %copy-done.1, f32[1536,512]{1,0:T(8,128)} %all-gather.5.cloned.1.call-done, f32[97,1536]{1,0:T(8,128)S(1)} %copy-done.2, f32[]{:T(128)} %bitcast.1, f32[1536]{0:T(1024)S(1)} %get-tuple-element.5, f32[96]{0:T(128)S(1)} %dynamic-slice_bitcast_fusion), kind=kOutput, calls=%fused_computation.12 | convolution fusion | flops 909115392 | bytes 5513732 | tf_op jit(solution)/shard_map/dot_general | solution.py:14
  (2 shorter events, 0.0 us)
Async XLA Ops:
  7.2 13.6 %copy-start = (f32[8192]{0:T(1024)S(1)}, f32[8192]{0:T(1024)}, u32[]{:S(2)}) copy-start(f32[8192]{0:T(1024)} %param.6) | copy-start | bytes 98308
  7.2 38.1 %all-gather.3.cloned.1.call-start = ((), (), s32[]{:S(2)}) async-start(), calls=%async_computation.3 | async-start | bytes 1671168 | tf_op jit(solution)/shard_map/all_gather | solution.py:23
  7.9 270.8 %reduce-scatter.2.cloned.1.call-start = ((), (), s32[]{:S(2)}) async-start(), calls=%async_computation.5 | async-start | bytes 3342336 | tf_op jit(solution)/shard_map/reduce_scatter | solution.py:42
  20.7 11.8 %copy-start.4 = (s32[2048]{0:T(1024)S(1)}, s32[2048]{0:T(1024)}, u32[]{:S(2)}) copy-start(s32[2048]{0:T(1024)} %param.7) | copy-start | bytes 24580
  214.0 1.4 copy-start.1
  214.0 1.8 copy-start.3
  214.0 152.2 %all-reduce.2.cloned.1.call-start = ((), (), s32[]{:S(2)}) async-start(), calls=%async_computation.4 | async-start | bytes 1277952 | tf_op jit(solution)/shard_map/psum | solution.py:29
  217.3 183.7 %all-gather.5.cloned.1.call-start = ((), (), s32[]{:S(2)}) async-start(), calls=%async_computation.6 | async-start | bytes 3342336 | tf_op jit(solution)/shard_map/all_gather | solution.py:41
  368.5 32.6 %copy-start.2 = (f32[97,1536]{1,0:T(8,128)S(1)}, f32[97,1536]{1,0:T(8,128)}, u32[]{:S(2)}) copy-start(f32[97,1536]{1,0:T(8,128)} %all-reduce.2.cloned.1.call-done) | copy-start | bytes 1787908
Sparse Core Ops, SparseCore 0:
  9.7 35.5 all-gather.2
  214.1 64.5 reduce-scatter.1
  281.2 84.9 all-reduce.1
  367.8 33.2 all-gather.4

commit v3 on v2

v3 whole, which is shorter than its diff:
```python
import jax
import jax.numpy as jnp
from jax import lax
from jax.sharding import PartitionSpec as P

NCH = 2


def contract(left, right):
    return lax.dot_general(
        left, right, (((1,), (1,)), ((), ())), preferred_element_type=jnp.float32
    )


def exact_dot(left, right):
    return jnp.dot(left, right, precision=lax.Precision.HIGHEST)


def step(dataset, targets, indices, particles, spread):
    n_feat = lax.axis_size("feat")
    batch_x = jnp.take(dataset, indices, axis=0)
    batch_t = jnp.take(targets, indices, axis=0)
    data_ratio = dataset.shape[0] / indices.shape[0]
    scale_h = spread[0].astype(jnp.float32)
    all_rows = lax.all_gather(particles, "dp", axis=0, tiled=True)
    count_all = all_rows.shape[0]
    rows_own = particles.shape[0]
    inner_part = contract(particles, all_rows)
    theta_all = all_rows.astype(jnp.float32)
    sq_part = jnp.sum(theta_all * theta_all, axis=1)
    packed = lax.psum(jnp.concatenate([inner_part, sq_part[None, :]], axis=0), "feat")
    inner = packed[:rows_own]
    norms_b = packed[rows_own]
    own_sq = lax.dynamic_slice_in_dim(norms_b, lax.axis_index("dp") * rows_own, rows_own, 0)
    kernel = jnp.exp(-(own_sq[:, None] + norms_b[None, :] - 2.0 * inner) / scale_h)
    chunk = count_all // NCH
    terms = []

    def issue_dp(c, grad_part):
        grad_own = lax.psum_scatter(grad_part, "dp", scatter_dimension=0, tiled=True)
        gradient = lax.all_gather(grad_own, "dp", axis=0, tiled=True)
        score = data_ratio * gradient - theta_all[c * chunk:(c + 1) * chunk]
        terms.append(exact_dot(kernel[:, c * chunk:(c + 1) * chunk], score))

    grad_part = None
    for c in range(NCH):
        rows_c = all_rows[c * chunk:(c + 1) * chunk]
        partial_t = contract(rows_c, batch_x).astype(jnp.bfloat16)
        if grad_part is not None:
            partial_t, grad_part = lax.optimization_barrier((partial_t, grad_part))
            issue_dp(c - 1, grad_part)
        partial_t = partial_t.reshape(n_feat, chunk // n_feat, partial_t.shape[1])
        pieces = lax.all_to_all(partial_t, "feat", 0, 0, tiled=True)
        own_logits_t = jnp.sum(pieces.astype(jnp.float32), axis=0)
        own_residual_t = (batch_t[None, :] - jax.nn.sigmoid(own_logits_t)).astype(jnp.bfloat16)
        spread_res = jnp.broadcast_to(own_residual_t[None], (n_feat,) + own_residual_t.shape)
        residual_t = lax.all_to_all(spread_res, "feat", 0, 0, tiled=True).reshape(chunk, -1)
        grad_part = jnp.dot(residual_t, batch_x, preferred_element_type=jnp.float32)
    issue_dp(NCH - 1, grad_part)
    pushed = terms[0]
    for term in terms[1:]:
        pushed = pushed + term
    pulled = exact_dot(kernel, theta_all)
    weight = jnp.sum(kernel, axis=1)
    attraction = pushed / count_all
    repulsion = (particles.astype(jnp.float32) * weight[:, None] - pulled) / count_all
    return attraction, repulsion


def solution(mesh):
    return jax.shard_map(
        step,
        mesh=mesh,
        in_specs=(P("dp", "feat"), P("dp"), P("dp"), P("dp", "feat"), P()),
        out_specs=(P("dp", "feat"), P("dp", "feat")),
        check_vma=False,
    )
```

time: 414 us -> 530 us (1.28)
  waiting for transfers between devices: 191 us -> 310 us
  blocking collectives: 156 us -> 132 us
  matrix products: 18.7 us -> 26.2 us
  local copies, waits for them, and re-layouts: 26.9 us -> 33.6 us
    reduce_scatter x1 -> x2, waiting for transfers between devices: 61.1 us -> 121 us  [issue_dp(): lax.psum_scatter(grad_part, 'dp', scatter_dimension=0, tiled=True)]
    all_to_all x0 -> x1, waiting for transfers between devices: none -> 31.1 us  [step(): lax.all_to_all(spread_res, 'feat', 0, 0, tiled=True).reshape(chunk, -1)]
    all_gather x2 -> x3, waiting for transfers between devices: 42.5 us -> 71.3 us  [the longest x2 60.2 us: issue_dp(): gradient = lax.all_gather(grad_own, 'dp', axis=0, tiled=True)]
    all_to_all x2 -> x3, blocking collectives: 156 us -> 132 us  [the longest x2 90.8 us: step(): pieces = lax.all_to_all(partial_t, 'feat', 0, 0, tiled=True)]
  transfers between devices with their start and end apart: 4 -> 7, of which waited for: 4 -> 7; matrix products, arithmetic and copies ran while one was open for 8% -> 8% of each run, Pallas kernels for 0% -> 0%
where the time goes in v3:
time: 530 us; the launch traced here: 528 us
  waiting for transfers between devices  310 us (58%)
  blocking collectives  132 us (25%)
  local copies, waits for them, and re-layouts  33.6 us (6%)
  matrix products  26.2 us (5%)
  between operations  14.9 us (3%)
  other arithmetic  7.04 us (1%)
    reduce_scatter x2, waiting for transfers between devices, issue_dp(): lax.psum_scatter(grad_part, 'dp', scatter_dimension=0, tiled=True)  121 us
    all_to_all x2, blocking collectives, step(): pieces = lax.all_to_all(partial_t, 'feat', 0, 0, tiled=True)  90.8 us
    psum x1, waiting for transfers between devices, step(): lax.psum(jnp.concatenate([inner_part, sq_part[None, :]], axis=0), 'feat')  84.5 us
    all_gather x2, waiting for transfers between devices, issue_dp(): gradient = lax.all_gather(grad_own, 'dp', axis=0, tiled=True)  60.2 us
    all_to_all x1, blocking collectives, step(): lax.all_to_all(spread_res, 'feat', 0, 0, tiled=True).reshape(chunk, -1)  41.3 us
    all_to_all x1, waiting for transfers between devices, step(): lax.all_to_all(spread_res, 'feat', 0, 0, tiled=True).reshape(chunk, -1)  31.1 us
    gather x1, local copies, waits for them, and re-layouts, step(): batch_x = jnp.take(dataset, indices, axis=0)  13.8 us
    gather x1, local copies, waits for them, and re-layouts, step(): batch_t = jnp.take(targets, indices, axis=0)  11.8 us
  transfers between devices with their start and end apart: 7, of which 7 were waited for; matrix products, arithmetic and copies ran while one was open for 8% of the time, Pallas kernels for 0%

profile of v3, /device:TPU:0, one launch (start us, length us, event | category | flops | bytes accessed | tf_op | source)
XLA Modules:
  0.0 528.5 jit_solution(5664039799077114109)
XLA Ops:
  7.2 0.0 copy-start
  7.2 0.0 all-gather.4.cloned.1.call-start
  7.2 0.7 all-gather.4.cloned.1.call-update
  7.9 0.7 fusion.18
  8.6 11.8 %gather_fusion.1 = f32[2048]{0:T(1024)S(1)} fusion(f32[8192]{0:T(1024)S(1)} %copy-done, s32[2048]{0:T(1024)S(1)} %fusion.18), kind=kCustom, calls=%fused_computation.1 | custom fusion | bytes 24576 | tf_op jit(solution)/shard_map/jit(_take)/gather | solution.py:22
  20.4 13.8 %gather_fusion = bf16[2048,512]{1,0:T(8,128)(2,1)} fusion(bf16[8192,512]{1,0:T(8,128)(2,1)} %param.5, s32[2048]{0:T(1024)S(1)} %fusion.18), kind=kCustom, calls=%fused_computation | custom fusion | bytes 4202496 | tf_op jit(solution)/shard_map/jit(_take)/gather | solution.py:21
  34.2 11.1 %all-gather.4.cloned.1.call-done = bf16[1536,512]{1,0:T(8,128)(2,1)} async-done(((bf16[96,512]{1,0:T(8,128)(2,1)}), bf16[1536,512]{1,0:T(8,128)(2,1)}) %all-gather.4.cloned.1.call-update) | async-done | bytes 1572880 | tf_op jit(solution)/shard_map/all_gather | solution.py:25
  45.3 3.7 convolution_convert_fusion
  49.0 46.2 %all_to_all.20 = bf16[8,96,2048]{2,1,0:T(8,128)(2,1)S(1)} all-to-all(bf16[8,96,2048]{2,1,0:T(8,128)(2,1)S(1)} %bitcast.19), channel_id=1, replica_groups=mesh['dp'=16,'feat'=8] {'feat'}, dimensions={0} | all-to-all | bytes 6291456 | tf_op jit(solution)/shard_map/all_to_all | solution.py:53
  95.2 0.6 convert_reduce_fusion.1
  95.8 0.2 subtract_convert_fusion.1
  96.0 2.1 broadcast_in_dim.42
  98.1 4.6 all-to-all-start.1
  102.7 0.0 reduce-scatter.5.cloned.1.call-start
  102.8 5.1 fusion
  107.9 31.1 %all-to-all-done.1 = bf16[8,96,2048]{2,1,0:T(8,128)(2,1)} async-done(((bf16[8,96,2048]{2,1,0:T(8,128)(2,1)}), bf16[8,96,2048]{2,1,0:T(8,128)(2,1)}, u32[]{:S(2)}, u32[]{:S(2)}) %all-to-all-start.1) | async-done | bytes 3145760 | tf_op jit(solution)/shard_map/all_to_all | solution.py:57
  138.9 5.5 %fusion.22 = f32[768,512]{1,0:T(8,128)} fusion(bf16[768,2048]{1,0:T(8,128)(2,1)} %bitcast.5, bf16[2048,512]{1,0:T(8,128)(2,1)} %gather_fusion, pred[2048]{0:T(1024)(128)(4,1)S(1)} %get-tuple-element.9), kind=kOutput, calls=%fused_computation.42 | convolution fusion | flops 1611661312 | bytes 6817792 | tf_op jit(solution)/shard_map/dot_general | solution.py:58
  144.5 4.7 copy.7
  149.1 44.5 %all_to_all.21 = bf16[8,96,2048]{2,1,0:T(8,128)(2,1)S(1)} all-to-all(bf16[8,96,2048]{2,1,0:T(8,128)(2,1)} %bitcast.17), channel_id=1, replica_groups=mesh['dp'=16,'feat'=8] {'feat'}, dimensions={0} | all-to-all | bytes 6291456 | tf_op jit(solution)/shard_map/all_to_all | solution.py:53
  193.7 0.6 convert_reduce_fusion
  194.2 0.2 subtract_convert_fusion
  194.5 0.4 broadcast_in_dim.43
  194.9 41.3 %all_to_all.22 = bf16[8,96,2048]{2,1,0:T(8,128)(2,1)S(1)} all-to-all(bf16[8,96,2048]{2,1,0:T(8,128)(2,1)S(1)} %broadcast_in_dim.43), channel_id=1, replica_groups=mesh['dp'=16,'feat'=8] {'feat'}, dimensions={0} | all-to-all | bytes 6291456 | tf_op jit(solution)/shard_map/all_to_all | solution.py:57
  236.2 3.0 fusion.21
  239.2 0.0 reduce-scatter.5.cloned.1.call-update
  239.2 0.0 reduce-scatter.3.cloned.1.call-start
  239.3 0.7 reduce-scatter.3.cloned.1.call-update
  240.0 0.2 all-reduce.2.cloned.1.call-start
  240.2 0.4 multiply_reduce_fusion
  240.6 0.6 fusion.26
  241.2 0.9 pad_maximum_fusion
  242.1 0.0 all-reduce.2.cloned.1.call-update
  242.2 0.0 all-gather.8.cloned.1.call-start
  242.2 57.1 %reduce-scatter.5.cloned.1.call-done = f32[48,512]{1,0:T(8,128)} async-done(((f32[768,512]{1,0:T(8,128)}), f32[48,512]{1,0:T(8,128)}) %reduce-scatter.5.cloned.1.call-update) | async-done | bytes 98320 | tf_op jit(solution)/shard_map/reduce_scatter | solution.py:40
  299.3 0.0 all-gather.8.cloned.1.call-update
  299.3 0.0 all-gather.6.cloned.1.call-start
  299.4 64.2 %reduce-scatter.3.cloned.1.call-done = f32[48,512]{1,0:T(8,128)} async-done(((f32[768,512]{1,0:T(8,128)}), f32[48,512]{1,0:T(8,128)}) %reduce-scatter.3.cloned.1.call-update) | async-done | bytes 98320 | tf_op jit(solution)/shard_map/reduce_scatter | solution.py:40
  363.5 0.0 all-gather.6.cloned.1.call-update
  364.2 2.1 convert_element_type.44
  366.3 84.5 %all-reduce.2.cloned.1.call-done = f32[97,1536]{1,0:T(8,128)} async-done(((f32[97,1536]{1,0:T(8,128)}), f32[97,1536]{1,0:T(8,128)}) %all-reduce.2.cloned.1.call-update) | async-done | bytes 595984 | tf_op jit(solution)/shard_map/psum | solution.py:31
  450.8 0.8 fusion.25
  451.7 0.1 dynamic-slice_bitcast_fusion
  451.7 1.4 fusion.23
  453.1 1.6 fusion.7
  454.7 28.7 %all-gather.8.cloned.1.call-done = f32[768,512]{1,0:T(8,128)} async-done(((f32[48,512]{1,0:T(8,128)}), f32[768,512]{1,0:T(8,128)}) %all-gather.8.cloned.1.call-update) | async-done | bytes 1572880 | tf_op jit(solution)/shard_map/all_gather | solution.py:41
  483.4 3.0 fusion.1
  486.4 31.5 %all-gather.6.cloned.1.call-done = f32[768,512]{1,0:T(8,128)} async-done(((f32[48,512]{1,0:T(8,128)}), f32[768,512]{1,0:T(8,128)}) %all-gather.6.cloned.1.call-update) | async-done | bytes 1572880 | tf_op jit(solution)/shard_map/all_gather | solution.py:41
  517.9 3.7 fusion.6
  (11 shorter events, 0.0 us)
Async XLA Ops:
  7.2 1.5 copy-start
  7.2 38.1 %all-gather.4.cloned.1.call-start = ((), (), s32[]{:S(2)}) async-start(), calls=%async_computation.6 | async-start | bytes 1671168 | tf_op jit(solution)/shard_map/all_gather | solution.py:25
  20.4 13.8 %copy-start.4 = (s32[2048]{0:T(1024)S(1)}, s32[2048]{0:T(1024)}, u32[]{:S(2)}) copy-start(s32[2048]{0:T(1024)} %param.7) | copy-start | bytes 24580
  98.1 4.6 copy-start.1
  98.1 40.8 %all-to-all-start.1 = ((bf16[8,96,2048]{2,1,0:T(8,128)(2,1)}), bf16[8,96,2048]{2,1,0:T(8,128)(2,1)}, u32[]{:S(2)}, u32[]{:S(2)}) async-start(bf16[8,96,2048]{2,1,0:T(8,128)(2,1)} %broadcast_in_dim.42), calls=%async_computation.1 | async-start | bytes 6291456 | tf_op jit(solution)/shard_map/all_to_all | solution.py:57
  102.7 196.6 %reduce-scatter.5.cloned.1.call-start = ((), (), s32[]{:S(2)}) async-start(), calls=%async_computation.10 | async-start | bytes 1671168 | tf_op jit(solution)/shard_map/reduce_scatter | solution.py:40
  194.9 41.3 %copy-start.2 = (bf16[2048,512]{1,0:T(8,128)(2,1)S(1)}, bf16[2048,512]{1,0:T(8,128)(2,1)}, u32[]{:S(2)}) copy-start(bf16[2048,512]{1,0:T(8,128)(2,1)} %gather_fusion) | copy-start | bytes 6291460
  239.2 1.4 copy-start.3
  239.2 124.3 %reduce-scatter.3.cloned.1.call-start = ((), (), s32[]{:S(2)}) async-start(), calls=%async_computation.8 | async-start | bytes 1671168 | tf_op jit(solution)/shard_map/reduce_scatter | solution.py:40
  240.0 210.9 %all-reduce.2.cloned.1.call-start = ((), (), s32[]{:S(2)}) async-start(), calls=%async_computation.7 | async-start | bytes 1277952 | tf_op jit(solution)/shard_map/psum | solution.py:31
  242.2 241.3 %all-gather.8.cloned.1.call-start = ((), (), s32[]{:S(2)}) async-start(), calls=%async_computation.11 | async-start | bytes 1671168 | tf_op jit(solution)/shard_map/all_gather | solution.py:41
  299.3 218.6 %all-gather.6.cloned.1.call-start = ((), (), s32[]{:S(2)}) async-start(), calls=%async_computation.9 | async-start | bytes 1671168 | tf_op jit(solution)/shard_map/all_gather | solution.py:41
Sparse Core Ops, SparseCore 0:
  9.7 35.5 all-gather.3
  239.4 59.8 reduce-scatter.4
  301.7 61.7 reduce-scatter.2
  365.9 84.8 all-reduce.1
  452.4 30.9 all-gather.7
  485.0 32.8 all-gather.5

commit v4 on v2

--- a/solution.py
+++ b/solution.py
@@ -14,7 +14,7 @@
     return jnp.dot(left, right, precision=lax.Precision.HIGHEST)
 
 
-def body(dataset, targets, indices, particles, spread):
+def step(dataset, targets, indices, particles, spread):
     n_feat = lax.axis_size("feat")
     batch_x = jnp.take(dataset, indices, axis=0)
     batch_t = jnp.take(targets, indices, axis=0)
@@ -26,22 +26,28 @@
     inner_part = contract(particles, all_rows)
     theta_all = all_rows.astype(jnp.float32)
     sq_part = jnp.sum(theta_all * theta_all, axis=1)
-    packed = lax.psum(jnp.concatenate([inner_part, sq_part[None, :]], axis=0), "feat")
-    inner = packed[:rows_own]
-    norms_b = packed[rows_own]
-    own_sq = lax.dynamic_slice_in_dim(norms_b, lax.axis_index("dp") * rows_own, rows_own, 0)
+    to_sum = jnp.concatenate([inner_part, sq_part[None, :]], axis=0)
     partial_t = contract(all_rows, batch_x).astype(jnp.bfloat16)
     partial_t = partial_t.reshape(n_feat, count_all // n_feat, partial_t.shape[1])
     pieces = lax.all_to_all(partial_t, "feat", 0, 0, tiled=True)
+    to_sum, pieces = lax.optimization_barrier((to_sum, pieces))
+    packed = lax.psum(to_sum, "feat")
     own_logits_t = jnp.sum(pieces.astype(jnp.float32), axis=0)
     own_residual_t = (batch_t[None, :] - jax.nn.sigmoid(own_logits_t)).astype(jnp.bfloat16)
     spread_res = jnp.broadcast_to(own_residual_t[None], (n_feat,) + own_residual_t.shape)
     residual_t = lax.all_to_all(spread_res, "feat", 0, 0, tiled=True).reshape(count_all, -1)
+    inner = packed[:rows_own]
+    norms_b = packed[rows_own]
+    own_sq = lax.dynamic_slice_in_dim(norms_b, lax.axis_index("dp") * rows_own, rows_own, 0)
     grad_part = jnp.dot(residual_t, batch_x, preferred_element_type=jnp.float32)
-    gradient = lax.all_gather(
-        lax.psum_scatter(grad_part, "dp", scatter_dimension=0, tiled=True),
-        "dp", axis=0, tiled=True,
+    n_dp = lax.axis_size("dp")
+    grad_pieces = lax.all_to_all(
+        grad_part.reshape(n_dp, rows_own, grad_part.shape[1]), "dp", 0, 0, tiled=True
     )
+    grad_own = jnp.sum(grad_pieces, axis=0)
+    gradient = lax.all_to_all(
+        jnp.broadcast_to(grad_own[None], (n_dp,) + grad_own.shape), "dp", 0, 0, tiled=True
+    ).reshape(count_all, -1)
     score = data_ratio * gradient - theta_all
     kernel = jnp.exp(-(own_sq[:, None] + norms_b[None, :] - 2.0 * inner) / scale_h)
     pushed = exact_dot(kernel, score)
@@ -54,7 +60,7 @@
 
 def solution(mesh):
     return jax.shard_map(
-        body,
+        step,
         mesh=mesh,
         in_specs=(P("dp", "feat"), P("dp"), P("dp"), P("dp", "feat"), P()),
         out_specs=(P("dp", "feat"), P("dp", "feat")),

time: 414 us -> 378 us (0.913)
  blocking collectives: 156 us -> 121 us
  waiting for transfers between devices: 191 us -> 170 us
  starting transfers between devices: 0.34 us -> 11.1 us
  other arithmetic: 4.98 us -> 12.5 us
    all_to_all x0 -> x2, waiting for transfers between devices: none -> 69.9 us  [the longest x1 69.9 us: step(): pieces = lax.all_to_all(partial_t, 'feat', 0, 0, tiled=True)]
    reduce_scatter x1 -> x0, waiting for transfers between devices: 61.1 us -> none  [body(): lax.psum_scatter(grad_part, 'dp', scatter_dimension=0, tiled=True)]
    all_to_all x2, blocking collectives: 156 us -> 121 us  [the longest x1 78.2 us: step(): lax.all_to_all(spread_res, 'feat', 0, 0, tiled=True).reshape(count_all, -1)]
    all_gather x2 -> x1, waiting for transfers between devices: 42.5 us -> 11.1 us  [step(): all_rows = lax.all_gather(particles, 'dp', axis=0, tiled=True)]
    all_to_all x0 -> x2, starting transfers between devices: none -> 11 us  [the longest x1 6.56 us: step(): pieces = lax.all_to_all(partial_t, 'feat', 0, 0, tiled=True)]
    reduce_sum x3 -> x4, other arithmetic: 2.95 us -> 8.12 us  [the longest x1 4.17 us: step(): own_logits_t = jnp.sum(pieces.astype(jnp.float32), axis=0)]
  transfers between devices with their start and end apart: 4 -> 4, of which waited for: 4 -> 3; matrix products, arithmetic and copies ran while one was open for 8% -> 9% of each run, Pallas kernels for 0% -> 0%
where the time goes in v4:
time: 378 us
  waiting for transfers between devices  170 us (45%)
  blocking collectives  121 us (32%)
  local copies, waits for them, and re-layouts  29.3 us (8%)
  matrix products  18.1 us (5%)
  between operations  14.8 us (4%)
  other arithmetic  12.5 us (3%)
  starting transfers between devices  11.1 us (3%)
    psum x1, waiting for transfers between devices, step(): packed = lax.psum(to_sum, 'feat')  88 us
    all_to_all x1, blocking collectives, step(): lax.all_to_all(spread_res, 'feat', 0, 0, tiled=True).reshape(count_all, -1)  78.2 us
    all_to_all x1, waiting for transfers between devices, step(): pieces = lax.all_to_all(partial_t, 'feat', 0, 0, tiled=True)  69.9 us
    all_to_all x1, blocking collectives, step(): lax.all_to_all(grad_part.reshape(n_dp, rows_own, grad_part.shape[1]), 'dp...  43.2 us
    gather x1, local copies, waits for them, and re-layouts, step(): batch_x = jnp.take(dataset, indices, axis=0)  13.7 us
    gather x1, local copies, waits for them, and re-layouts, step(): batch_t = jnp.take(targets, indices, axis=0)  11.8 us
    all_gather x1, waiting for transfers between devices, step(): all_rows = lax.all_gather(particles, 'dp', axis=0, tiled=True)  11.1 us
    dot_general x2, matrix products, contract(): lax.dot_general(left, right, (((1,), (1,)), ((), ())), preferred_element_...  8.86 us
  transfers between devices with their start and end apart: 4, of which 3 were waited for; matrix products, arithmetic and copies ran while one was open for 9% of the time, Pallas kernels for 0%

profile of v4, /device:TPU:0, one launch (start us, length us, event | category | flops | bytes accessed | tf_op | source)
XLA Modules:
  0.0 377.7 jit_solution(16045815999714405887)
XLA Ops:
  7.2 0.0 copy-start
  7.2 0.0 all-gather.2.cloned.1.call-start
  7.2 0.7 all-gather.2.cloned.1.call-update
  7.9 0.7 fusion.10
  8.6 13.7 %gather_fusion = bf16[2048,512]{1,0:T(8,128)(2,1)} fusion(bf16[8192,512]{1,0:T(8,128)(2,1)} %param.5, s32[2048]{0:T(1024)S(1)} %fusion.10), kind=kCustom, calls=%fused_computation | custom fusion | bytes 4202496 | tf_op jit(solution)/shard_map/jit(_take)/gather | solution.py:19
  22.4 0.0 copy-done
  22.4 0.0 copy-start.5
  22.4 11.8 %gather_fusion.1 = f32[2048]{0:T(1024)S(1)} fusion(f32[8192]{0:T(1024)S(1)} %copy-done, s32[2048]{0:T(1024)S(1)} %fusion.10), kind=kCustom, calls=%fused_computation.1 | custom fusion | bytes 24576 | tf_op jit(solution)/shard_map/jit(_take)/gather | solution.py:20
  34.1 0.0 copy-done.5
  34.2 11.1 %all-gather.2.cloned.1.call-done = bf16[1536,512]{1,0:T(8,128)(2,1)} async-done(((bf16[96,512]{1,0:T(8,128)(2,1)}), bf16[1536,512]{1,0:T(8,128)(2,1)}) %all-gather.2.cloned.1.call-update) | async-done | bytes 1572880 | tf_op jit(solution)/shard_map/all_gather | solution.py:23
  45.3 8.3 %convolution_convert_fusion = bf16[2048,1536]{0,1:T(8,128)(2,1)} fusion(bf16[1536,512]{1,0:T(8,128)(2,1)} %all-gather.2.cloned.1.call-done, bf16[2048,512]{1,0:T(8,128)(2,1)} %gather_fusion, pred[2048]{0:T(1024)(128)(4,1)S(1)} %get-tuple-element.7), kind=kOutput, calls=%fused_computation.3 | convolution fusion | flops 3225419776 | bytes 9963520 | tf_op jit(solution)/shard_map/dot_general | solution.py:8
  53.6 0.0 copy-start.1
  53.6 0.0 copy-start.4
  53.6 6.6 %all-to-all-start = ((bf16[8,192,2048]{2,1,0:T(8,128)(2,1)}), bf16[8,192,2048]{2,1,0:T(8,128)(2,1)}, u32[]{:S(2)}, u32[]{:S(2)}) async-start(bf16[8,192,2048]{2,1,0:T(8,128)(2,1)} %bitcast.17), calls=%async_computation | async-start | bytes 12582912 | tf_op jit(solution)/shard_map/all_to_all | solution.py:32
  60.1 0.0 copy-done.1
  60.2 0.4 fusion
  60.5 0.0 copy-done.4
  60.6 0.6 fusion.17
  61.2 0.9 pad_maximum_fusion
  62.1 69.9 %all-to-all-done = bf16[8,192,2048]{2,1,0:T(8,128)(2,1)} async-done(((bf16[8,192,2048]{2,1,0:T(8,128)(2,1)}), bf16[8,192,2048]{2,1,0:T(8,128)(2,1)}, u32[]{:S(2)}, u32[]{:S(2)}) %all-to-all-start) | async-done | bytes 6291488 | tf_op jit(solution)/shard_map/all_to_all | solution.py:32
  132.0 4.2 %convert_reduce_fusion = f32[192,2048]{1,0:T(8,128)S(1)} fusion(bf16[8,192,2048]{2,1,0:T(8,128)(2,1)} %all-to-all-done), kind=kLoop, calls=%fused_computation.2 | loop fusion | flops 5898240 | bytes 7864320 | tf_op jit(solution)/shard_map/reduce_sum | solution.py:35
  136.2 0.4 subtract_convert_fusion
  136.6 0.8 broadcast_in_dim.41
  137.4 0.0 copy-start.3
  137.4 78.2 %all_to_all.20 = bf16[8,192,2048]{2,1,0:T(8,128)(2,1)S(1)} all-to-all(bf16[8,192,2048]{2,1,0:T(8,128)(2,1)S(1)} %broadcast_in_dim.41), channel_id=1, replica_groups=mesh['dp'=16,'feat'=8] {'feat'}, dimensions={0} | all-to-all | bytes 12582912 | tf_op jit(solution)/shard_map/all_to_all | solution.py:38
  215.6 0.0 copy-done.3
  215.6 3.5 fusion.2
  219.1 43.2 %all_to_all.21 = f32[16,96,512]{2,1,0:T(8,128)} all-to-all(f32[16,96,512]{2,1,0:T(8,128)S(1)} %fusion.2), channel_id=1, replica_groups=mesh['dp'=16,'feat'=8] {'dp'}, dimensions={0} | all-to-all | bytes 6291456 | tf_op jit(solution)/shard_map/all_to_all | solution.py:44
  262.3 2.2 reduce_sum.38
  264.5 2.1 broadcast_in_dim.42
  266.6 4.5 %all-to-all-start.3 = ((f32[16,96,512]{2,1,0:T(8,128)}), f32[16,96,512]{2,1,0:T(8,128)}, u32[]{:S(2)}, u32[]{:S(2)}) async-start(f32[16,96,512]{2,1,0:T(8,128)} %broadcast_in_dim.42), calls=%async_computation.3 | async-start | bytes 6291456 | tf_op jit(solution)/shard_map/all_to_all | solution.py:48
  271.1 0.0 all-reduce.2.cloned.1.call-start
  271.1 0.7 all-reduce.2.cloned.1.call-update
  272.5 88.0 %all-reduce.2.cloned.1.call-done = f32[97,1536]{1,0:T(8,128)} async-done(((f32[97,1536]{1,0:T(8,128)}), f32[97,1536]{1,0:T(8,128)}) %all-reduce.2.cloned.1.call-update) | async-done | bytes 595984 | tf_op jit(solution)/shard_map/psum | solution.py:34
  360.5 0.8 fusion.16
  361.4 0.1 dynamic-slice_bitcast_fusion
  361.4 1.4 fusion.14
  362.8 2.7 fusion.5
  365.6 0.0 copy-start.2
  365.6 0.0 all-to-all-done.3
  365.6 2.3 broadcast_multiply_fusion
  367.9 0.0 copy-done.2
  367.9 3.0 fusion.4
  (2 shorter events, 0.0 us)
Async XLA Ops:
  7.2 15.2 %copy-start = (f32[8192]{0:T(1024)S(1)}, f32[8192]{0:T(1024)}, u32[]{:S(2)}) copy-start(f32[8192]{0:T(1024)} %param.6) | copy-start | bytes 98308
  7.2 38.1 %all-gather.2.cloned.1.call-start = ((), (), s32[]{:S(2)}) async-start(), calls=%async_computation.4 | async-start | bytes 1671168 | tf_op jit(solution)/shard_map/all_gather | solution.py:23
  22.4 11.8 %copy-start.5 = (s32[2048]{0:T(1024)S(1)}, s32[2048]{0:T(1024)}, u32[]{:S(2)}) copy-start(s32[2048]{0:T(1024)} %param.7) | copy-start | bytes 24580
  53.6 6.6 %copy-start.1 = (bf16[1536,512]{1,0:T(8,128)(2,1)S(1)}, bf16[1536,512]{1,0:T(8,128)(2,1)}, u32[]{:S(2)}) copy-start(bf16[1536,512]{1,0:T(8,128)(2,1)} %all-gather.2.cloned.1.call-done) | copy-start | bytes 4718596
  53.6 7.0 %copy-start.4 = (bf16[96,512]{1,0:T(8,128)(2,1)S(1)}, bf16[96,512]{1,0:T(8,128)(2,1)}, u32[]{:S(2)}) copy-start(bf16[96,512]{1,0:T(8,128)(2,1)} %param.8) | copy-start | bytes 294916
  53.6 78.4 %all-to-all-start = ((bf16[8,192,2048]{2,1,0:T(8,128)(2,1)}), bf16[8,192,2048]{2,1,0:T(8,128)(2,1)}, u32[]{:S(2)}, u32[]{:S(2)}) async-start(bf16[8,192,2048]{2,1,0:T(8,128)(2,1)} %bitcast.17), calls=%async_computation | async-start | bytes 12582912 | tf_op jit(solution)/shard_map/all_to_all | solution.py:32
  137.4 78.2 %copy-start.3 = (bf16[2048,512]{1,0:T(8,128)(2,1)S(1)}, bf16[2048,512]{1,0:T(8,128)(2,1)}, u32[]{:S(2)}) copy-start(bf16[2048,512]{1,0:T(8,128)(2,1)} %gather_fusion) | copy-start | bytes 6291460
  266.6 99.0 %all-to-all-start.3 = ((f32[16,96,512]{2,1,0:T(8,128)}), f32[16,96,512]{2,1,0:T(8,128)}, u32[]{:S(2)}, u32[]{:S(2)}) async-start(f32[16,96,512]{2,1,0:T(8,128)} %broadcast_in_dim.42), calls=%async_computation.3 | async-start | bytes 6291456 | tf_op jit(solution)/shard_map/all_to_all | solution.py:48
  271.1 89.4 %all-reduce.2.cloned.1.call-start = ((), (), s32[]{:S(2)}) async-start(), calls=%async_computation.5 | async-start | bytes 1277952 | tf_op jit(solution)/shard_map/psum | solution.py:34
  365.6 2.3 copy-start.2
Sparse Core Ops, SparseCore 0:
  9.7 35.5 all-gather.1
  274.4 86.0 all-reduce.1
